TPU v7x, 256 devices: a whole 4x4x8 slice. The times are simulated.
256 devices in a mesh: lat: 16 (over y_lo, z), lon: 16 (over y_hi, x, core).
Axes of the slice: x: 4, y: 4 (y_hi: 2, y_lo: 2; y = y_hi * 2 + y_lo), z: 8, core: 2. Of those that a mesh axis runs over, the one named last changes fastest.
Arguments:
- prognostic: float32 [6, 2, 2304, 2048], P(None, None, 'lon', 'lat'), may hold values from -6 to 6
- wind_zonal: float32 [2, 2048], P(None, 'lat'), may hold values from -1 to 1
- wind_merid: float32 [2, 2048], P(None, 'lat'), may hold values from -0.5 to 0.5
- layer_depth: float32 [2], replicated, may hold values from 0.25 to 1
- diffusion: float32 [3, 2], replicated, may hold values from 0.05 to 0.4
Outputs:
- prognostic_out: float32 [6, 2, 2304, 2048], P(None, None, 'lon', 'lat')
All inputs are finite; a program needn't handle non-finite values.
Results may differ from a plain program's by a relative error of at most 0.00013.
Values sent between devices are 32-bit elements; how exact they have to be, the bound alone decides.
No kernel may reach another device: no remote copies, remote signals or barrier semaphores. Data moves between devices by JAX's collectives and lax.ppermute only.
A program may use at most 128 MiB of HBM per device.

v0:
```python
import math
import jax
import jax.numpy as jnp
from jax import lax
from jax.sharding import PartitionSpec as P

ITERS = 3
time_step = 0.15
highest = lax.Precision.HIGHEST


def with_halo(block, sides, width, periodic):
    for axis, dim in sides:
        count = lax.axis_size(axis)
        forward = [(i, i + 1) for i in range(count - 1)]
        if periodic:
            forward.append((count - 1, 0))
        backward = [(target, source) for source, target in forward]
        low = lax.ppermute(
            lax.slice_in_dim(block, block.shape[dim] - width, None, axis=dim), axis, forward
        )
        high = lax.ppermute(lax.slice_in_dim(block, 0, width, axis=dim), axis, backward)
        block = jnp.concatenate([low, block, high], axis=dim)
    return block


def latitude(row_ids, lat_total):
    return (row_ids.astype(jnp.float32) + 0.5) * (math.pi / lat_total) - 0.5 * math.pi


def damping(row_ids, lat_total, circle_len):
    cos_ratio = jnp.cos(latitude(row_ids, lat_total)) / math.cos(0.25 * math.pi)
    wave_ids = jnp.arange(circle_len // 2 + 1)
    sine_vals = jnp.sin(wave_ids.astype(jnp.float32) * (math.pi / circle_len))
    safe_sines = jnp.where(wave_ids == 0, 1.0, sine_vals)
    return jnp.where(
        wave_ids[None, :] == 0, 1.0, jnp.minimum(1.0, cos_ratio[:, None] / safe_sines[None, :])
    )


def tendency(
    fields_now,
    north_rows,
    south_rows,
    east_cols,
    west_cols,
    row_ids,
    lat_total,
    wind_zonal,
    wind_merid,
    layer_depth,
    diffusion,
):
    latitudes = latitude(row_ids, lat_total)
    cos_centre = jnp.cos(latitudes)
    cos_north = jnp.cos(latitude(row_ids + 1, lat_total))
    cos_south = jnp.cos(latitude(row_ids - 1, lat_total))
    coriolis = jnp.sin(latitudes)
    zonal_diff = (east_cols - west_cols) / (2.0 * cos_centre)
    merid_diff = 0.5 * (north_rows - south_rows)
    advect = wind_zonal[:, None, :] * zonal_diff + wind_merid[:, None, :] * merid_diff
    diverge = zonal_diff[0] + (north_rows[1] * cos_north - south_rows[1] * cos_south) / (
        2.0 * cos_centre
    )
    zonal_tend = -advect[0] + coriolis * fields_now[1] - zonal_diff[2]
    merid_tend = -advect[1] - coriolis * fields_now[0] - merid_diff[2]
    height_tend = -advect[2] - layer_depth[:, None, None] * diverge
    tracer_tend = -advect[3:] + diffusion[:, :, None, None] * (
        north_rows[3:] - 2.0 * fields_now[3:] + south_rows[3:]
    )
    return jnp.concatenate(
        [zonal_tend[None], merid_tend[None], height_tend[None], tracer_tend], axis=0
    )


def split_length(total):
    first = int(math.isqrt(total))
    while total % first != 0:
        first = first - 1
    return (first, total // first)


def trig_table(length):
    counts = jnp.arange(length, dtype=jnp.int32)
    phases = counts[:, None] * counts[None, :] % length
    angles = phases.astype(jnp.float32) * (2.0 * math.pi / length)
    return (jnp.cos(angles), jnp.sin(angles))


def twist_table(outer, inner, total):
    outer_ids = jnp.arange(outer, dtype=jnp.int32)
    inner_ids = jnp.arange(inner, dtype=jnp.int32)
    angles = (outer_ids[:, None] * inner_ids[None, :] % total).astype(jnp.float32) * (
        2.0 * math.pi / total
    )
    return (jnp.cos(angles)[None], jnp.sin(angles)[None])


def forward_real(signal):
    vectors, total = signal.shape
    inner, outer = split_length(total)
    grid = signal.reshape(vectors, outer, inner)
    cos_outer, sin_outer = trig_table(outer)
    first_re = jnp.einsum("mba,bk->mka", grid, cos_outer, precision=highest)
    first_im = -jnp.einsum("mba,bk->mka", grid, sin_outer, precision=highest)
    twist_cos, twist_sin = twist_table(outer, inner, total)
    mid_re = first_re * twist_cos + first_im * twist_sin
    mid_im = first_im * twist_cos - first_re * twist_sin
    cos_inner, sin_inner = trig_table(inner)
    last_re = jnp.einsum("mka,aq->mqk", mid_re, cos_inner, precision=highest) + jnp.einsum(
        "mka,aq->mqk", mid_im, sin_inner, precision=highest
    )
    last_im = jnp.einsum("mka,aq->mqk", mid_im, cos_inner, precision=highest) - jnp.einsum(
        "mka,aq->mqk", mid_re, sin_inner, precision=highest
    )
    return (last_re.reshape(vectors, total), last_im.reshape(vectors, total))


def inverse_real(spec_re, spec_im):
    vectors, total = spec_re.shape
    inner, outer = split_length(total)
    grid_re = spec_re.reshape(vectors, outer, inner)
    grid_im = spec_im.reshape(vectors, outer, inner)
    cos_outer, sin_outer = trig_table(outer)
    first_re = jnp.einsum("mba,bk->mka", grid_re, cos_outer, precision=highest) - jnp.einsum(
        "mba,bk->mka", grid_im, sin_outer, precision=highest
    )
    first_im = jnp.einsum("mba,bk->mka", grid_im, cos_outer, precision=highest) + jnp.einsum(
        "mba,bk->mka", grid_re, sin_outer, precision=highest
    )
    twist_cos, twist_sin = twist_table(outer, inner, total)
    mid_re = first_re * twist_cos - first_im * twist_sin
    mid_im = first_im * twist_cos + first_re * twist_sin
    cos_inner, sin_inner = trig_table(inner)
    last_re = jnp.einsum("mka,aq->mqk", mid_re, cos_inner, precision=highest) - jnp.einsum(
        "mka,aq->mqk", mid_im, sin_inner, precision=highest
    )
    return last_re.reshape(vectors, total)


def local(prognostic, wind_zonal, wind_merid, layer_depth, diffusion):
    field_count, level_count, col_count, row_count = prognostic.shape
    lat_devs = lax.axis_size("lat")
    lon_devs = lax.axis_size("lon")
    lat_total = row_count * lat_devs
    circle_len = col_count * lon_devs
    lat_pos = lax.axis_index("lat")
    lon_pos = lax.axis_index("lon")
    row_ids = lat_pos * row_count + jnp.arange(row_count, dtype=jnp.int32)
    quarter = lat_devs // 4
    is_polar = (lat_pos < quarter) | (lat_pos >= lat_devs - quarter)

    def smooth(sector, start_row):
        vectors, total, slab_rows = sector.shape
        halfway = damping(start_row + jnp.arange(slab_rows, dtype=jnp.int32), lat_total, circle_len)
        mirrored = halfway[:, 1 : circle_len // 2][:, ::-1]
        factors = jnp.concatenate([halfway, mirrored], axis=1)[None]
        rows_last = jnp.transpose(sector, (0, 2, 1)).reshape(vectors * slab_rows, total)
        spec_re, spec_im = forward_real(rows_last)
        spec_re = (spec_re.reshape(vectors, slab_rows, total) * factors).reshape(
            vectors * slab_rows, total
        )
        spec_im = (spec_im.reshape(vectors, slab_rows, total) * factors).reshape(
            vectors * slab_rows, total
        )
        back = inverse_real(spec_re, spec_im) * (1.0 / circle_len)
        return jnp.transpose(back.reshape(vectors, slab_rows, total), (0, 2, 1))

    fields_now = prognostic
    for substep in range(ITERS):
        lat_padded = with_halo(fields_now, (("lat", 3),), 1, False)
        lon_padded = with_halo(fields_now, (("lon", 2),), 1, True)
        tendency_now = tendency(
            fields_now,
            lat_padded[:, :, :, 2:],
            lat_padded[:, :, :, :-2],
            lon_padded[:, :, 2:],
            lon_padded[:, :, :-2],
            row_ids,
            lat_total,
            wind_zonal,
            wind_merid,
            layer_depth,
            diffusion,
        )
        flattened = tendency_now.reshape(field_count * level_count, col_count, row_count)

        def filter_sector(sector):
            slab_rows = sector.shape[2]
            start_row = lat_pos * row_count + lon_pos * slab_rows
            damped = lax.cond(
                is_polar, lambda inner: smooth(inner, start_row), lambda inner: inner, sector
            )
            return lax.all_to_all(damped, "lon", split_axis=1, concat_axis=2, tiled=True)

        filtered = filter_sector(
            lax.all_to_all(flattened, "lon", split_axis=2, concat_axis=1, tiled=True)
        )
        fields_now = fields_now + time_step * filtered.reshape(fields_now.shape)
    return fields_now


def solution(mesh):
    return jax.shard_map(
        local,
        mesh=mesh,
        in_specs=(P(None, None, "lon", "lat"), P(None, "lat"), P(None, "lat"), P(), P()),
        out_specs=P(None, None, "lon", "lat"),
        check_vma=False,
    )
```

profile of v0, /device:TPU:96, one launch (start us, length us, event | category | flops | bytes accessed | tf_op | source)
XLA Modules:
  0.0 506.7 jit_solution(1772880354401610135)
XLA Ops:
  32.9 16.2 %all-to-all-done = f32[16,1,13824]{2,1,0:T(1,128)S(1)} async-done(((f32[16,1,13824]{2,1,0:T(1,128)}), f32[16,1,13824]{2,1,0:T(1,128)S(1)}, u32[]{:S(2)}, u32[]{:S(2)}) %all-to-all-start) | async-done | bytes 884768 | tf_op jit(solution)/shard_map/all_to_all | solution.py:197
  63.1 36.6 %conditional.3 = (f32[12,2304,8]{1,2,0:T(8,128)S(1)}) conditional(s32[]{:T(128)} %convert_element_type.240, f32[12,2304,8]{1,2,0:T(8,128)S(1)} %all_to_all.72, (f32[12,2304,8]{1,2,0:T(8,128)S(1)}, s32[]{:T(128)}) %tuple.23), branch_computations={%region_0.0_spmd, %region_1.2_spmd} | conditional | flops 1533790208 | bytes 46552336 | solution.py:191
  99.8 5.4 %copy.262 = f32[12,2304,8]{0,2,1:T(8,128)} copy(f32[12,2304,8]{1,2,0:T(8,128)S(1)} %get-tuple-element.85) | data formatting | bytes 1769472 | tf_op jit(solution)/shard_map/cond | solution.py:191
  105.2 10.5 %reshape.288 = f32[16,1,13824]{2,1,0:T(1,128)S(1)} reshape(f32[2304,8,12]{2,1,0:T(8,128)} %bitcast.230) | data formatting | bytes 1769472
  115.7 19.3 %all_to_all.90 = f32[16,1,13824]{2,1,0:T(1,128)} all-to-all(f32[16,1,13824]{2,1,0:T(1,128)S(1)} %reshape.288), channel_id=1, replica_groups=mesh['lat'=16,'lon'=16] {'lon'}, dimensions={0} | all-to-all | bytes 1769472 | tf_op jit(solution)/shard_map/all_to_all | solution.py:194
  138.9 14.7 %reshape.289 = f32[2304,8,12]{2,1,0:T(8,128)} reshape(f32[16,13824]{1,0:T(8,128)S(1)} %reduce.1) | data formatting | bytes 1769472
  153.6 8.5 %broadcast_multiply_fusion.2 = f32[12,2304,8]{0,2,1:T(8,128)} fusion(f32[2304,8,12]{2,1,0:T(8,128)} %reshape.289), kind=kLoop, calls=%fused_computation.377 | loop fusion | flops 221184 | bytes 1769472 | tf_op jit(solution)/shard_map/mul | solution.py:199
  162.0 8.1 %copy.263 = f32[12,16,144,8]{2,3,1,0:T(8,128)} copy(f32[12,16,144,8]{0,3,2,1:T(8,128)} %bitcast.231) | data formatting | bytes 1769472 | tf_op jit(solution)/shard_map/mul | solution.py:199
  197.0 20.3 %all_to_all.91 = f32[16,1,13824]{2,1,0:T(1,128)} all-to-all(f32[16,1,13824]{2,1,0:T(1,128)S(1)} %reshape.290), channel_id=1, replica_groups=mesh['lat'=16,'lon'=16] {'lon'}, dimensions={0} | all-to-all | bytes 1769472 | tf_op jit(solution)/shard_map/all_to_all | solution.py:197
  229.6 36.6 %conditional.4 = (f32[12,2304,8]{1,2,0:T(8,128)S(1)}) conditional(s32[]{:T(128)} %convert_element_type.240, f32[12,2304,8]{1,2,0:T(8,128)S(1)} %all_to_all.77, (f32[12,2304,8]{1,2,0:T(8,128)S(1)}, s32[]{:T(128)}) %tuple.24), branch_computations={%region_2.3_spmd, %region_3.4_spmd} | conditional | flops 1533790208 | bytes 46552336 | solution.py:191
  266.3 5.4 %copy.272 = f32[12,2304,8]{0,2,1:T(8,128)} copy(f32[12,2304,8]{1,2,0:T(8,128)S(1)} %get-tuple-element.86) | data formatting | bytes 1769472 | tf_op jit(solution)/shard_map/cond | solution.py:191
  271.7 10.5 %reshape.292 = f32[16,1,13824]{2,1,0:T(1,128)S(1)} reshape(f32[2304,8,12]{2,1,0:T(8,128)} %bitcast.232) | data formatting | bytes 1769472
  282.2 19.3 %all_to_all.92 = f32[16,1,13824]{2,1,0:T(1,128)} all-to-all(f32[16,1,13824]{2,1,0:T(1,128)S(1)} %reshape.292), channel_id=1, replica_groups=mesh['lat'=16,'lon'=16] {'lon'}, dimensions={0} | all-to-all | bytes 1769472 | tf_op jit(solution)/shard_map/all_to_all | solution.py:194
  305.4 14.7 %reshape.293 = f32[2304,8,12]{2,1,0:T(8,128)} reshape(f32[16,13824]{1,0:T(8,128)S(1)} %reduce.3) | data formatting | bytes 1769472
  320.1 8.5 %broadcast_multiply_fusion.1 = f32[12,2304,8]{0,2,1:T(8,128)} fusion(f32[2304,8,12]{2,1,0:T(8,128)} %reshape.293), kind=kLoop, calls=%fused_computation.376 | loop fusion | flops 221184 | bytes 1769472 | tf_op jit(solution)/shard_map/mul | solution.py:199
  328.6 8.1 %copy.273 = f32[12,16,144,8]{2,3,1,0:T(8,128)} copy(f32[12,16,144,8]{0,3,2,1:T(8,128)} %bitcast.233) | data formatting | bytes 1769472 | tf_op jit(solution)/shard_map/mul | solution.py:199
  363.8 20.3 %all_to_all.93 = f32[16,1,13824]{2,1,0:T(1,128)} all-to-all(f32[16,1,13824]{2,1,0:T(1,128)S(1)} %reshape.294), channel_id=1, replica_groups=mesh['lat'=16,'lon'=16] {'lon'}, dimensions={0} | all-to-all | bytes 1769472 | tf_op jit(solution)/shard_map/all_to_all | solution.py:197
  396.4 36.5 %conditional.5 = (f32[12,2304,8]{1,2,0:T(8,128)S(1)}) conditional(s32[]{:T(128)} %convert_element_type.240, f32[12,2304,8]{1,2,0:T(8,128)S(1)} %all_to_all.82, (f32[12,2304,8]{1,2,0:T(8,128)S(1)}, s32[]{:T(128)}) %tuple.25), branch_computations={%region_4.5_spmd, %region_5.6_spmd} | conditional | flops 1533790208 | bytes 46552336 | solution.py:191
  432.9 5.4 %copy.281 = f32[12,2304,8]{0,2,1:T(8,128)} copy(f32[12,2304,8]{1,2,0:T(8,128)S(1)} %get-tuple-element.87) | data formatting | bytes 1769472 | tf_op jit(solution)/shard_map/cond | solution.py:191
  438.3 10.5 %reshape.296 = f32[16,1,13824]{2,1,0:T(1,128)S(1)} reshape(f32[2304,8,12]{2,1,0:T(8,128)} %bitcast.234) | data formatting | bytes 1769472
  448.9 19.3 %all_to_all.94 = f32[16,1,13824]{2,1,0:T(1,128)} all-to-all(f32[16,1,13824]{2,1,0:T(1,128)S(1)} %reshape.296), channel_id=1, replica_groups=mesh['lat'=16,'lon'=16] {'lon'}, dimensions={0} | all-to-all | bytes 1769472 | tf_op jit(solution)/shard_map/all_to_all | solution.py:194
  472.0 14.7 %reshape.297 = f32[2304,8,12]{2,1,0:T(8,128)} reshape(f32[16,13824]{1,0:T(8,128)S(1)} %reduce.5) | data formatting | bytes 1769472
  486.7 8.5 %broadcast_multiply_fusion = f32[12,2304,8]{0,2,1:T(8,128)} fusion(f32[2304,8,12]{2,1,0:T(8,128)} %reshape.297), kind=kLoop, calls=%fused_computation.375 | loop fusion | flops 221184 | bytes 1769472 | tf_op jit(solution)/shard_map/mul | solution.py:199
  495.2 8.1 %copy.282 = f32[12,16,144,8]{2,3,1,0:T(8,128)} copy(f32[12,16,144,8]{0,3,2,1:T(8,128)} %bitcast.235) | data formatting | bytes 1769472 | tf_op jit(solution)/shard_map/mul | solution.py:199
  (183 shorter events, 247.9 us)
Async XLA Ops:
  0.8 15.7 %collective-permute-start.1 = (f32[6,2,1,128]{3,1,2,0:T(2,128)S(1)}, f32[6,2,1,128]{3,1,2,0:T(2,128)S(1)}, u32[]{:S(2)}, u32[]{:S(2)}) collective-permute-start(f32[6,2,1,128]{3,1,2,0:T(2,128)S(1)} %bitcast.257), channel_id=1, source_target_pairs={{0,1},{1,2},{2,3},{3,4},{4,5},{5,6},{6,7},{7,8},{8,9},{9,10},{10,1... | collective-permute-start | bytes 18440 | tf_op jit(solution)/shard_map/ppermute | solution.py:19
  0.9 14.2 %copy-start.6 = (f32[2,128]{1,0:T(2,128)S(1)}, f32[2,128]{1,0:T(2,128)}, u32[]{:S(2)}) copy-start(f32[2,128]{1,0:T(2,128)} %param.13) | copy-start | bytes 3076
  0.9 14.3 %copy-start.5 = (f32[3,2]{0,1:T(2,128)S(1)}, f32[3,2]{0,1:T(2,128)}, u32[]{:S(2)}) copy-start(f32[3,2]{0,1:T(2,128)} %param.15) | copy-start | bytes 76
  1.0 14.4 %collective-permute-start = (f32[6,2,1,128]{3,1,2,0:T(2,128)S(1)}, f32[6,2,1,128]{3,1,2,0:T(2,128)S(1)}, u32[]{:S(2)}, u32[]{:S(2)}) collective-permute-start(f32[6,2,1,128]{3,1,2,0:T(2,128)S(1)} %bitcast.258), channel_id=1, source_target_pairs={{1,0},{2,1},{3,2},{4,3},{5,4},{6,5},{7,6},{8,7},{9,8},{10,9},{11,1... | collective-permute-start | bytes 18440 | tf_op jit(solution)/shard_map/ppermute | solution.py:22
  7.9 9.8 %copy-start.3 = (f32[2,128]{1,0:T(2,128)S(1)}, f32[2,128]{1,0:T(2,128)}, u32[]{:S(2)}) copy-start(f32[2,128]{1,0:T(2,128)} %param.12) | copy-start | bytes 3076
  8.0 9.8 %collective-permute-start.2 = (f32[6,2,144,1]{2,3,1,0:T(1,128)S(1)}, f32[6,2,144,1]{2,3,1,0:T(1,128)S(1)}, u32[]{:S(2)}, u32[]{:S(2)}) collective-permute-start(f32[6,2,144,1]{2,3,1,0:T(1,128)S(1)} %get-tuple-element.79), channel_id=1, source_target_pairs={{16,0},{32,16},{48,32},{64,48},{80,64},{96,80},{112,96},{128,112},... | collective-permute-start | bytes 20744 | tf_op jit(solution)/shard_map/ppermute | solution.py:22
  10.0 7.7 %collective-permute-start.3 = (f32[6,2,144,1]{2,3,1,0:T(1,128)S(1)}, f32[6,2,144,1]{2,3,1,0:T(1,128)S(1)}, u32[]{:S(2)}, u32[]{:S(2)}) collective-permute-start(f32[6,2,144,1]{2,3,1,0:T(1,128)S(1)} %get-tuple-element.80), channel_id=1, source_target_pairs={{0,16},{16,32},{32,48},{48,64},{64,80},{80,96},{96,112},{112,128},... | collective-permute-start | bytes 20744 | tf_op jit(solution)/shard_map/ppermute | solution.py:19
  20.6 0.7 copy-start.4
  27.8 21.3 %all-to-all-start = ((f32[16,1,13824]{2,1,0:T(1,128)}), f32[16,1,13824]{2,1,0:T(1,128)S(1)}, u32[]{:S(2)}, u32[]{:S(2)}) async-start(f32[16,1,13824]{2,1,0:T(1,128)} %reshape.286), calls=%async_computation | async-start | bytes 1769472 | tf_op jit(solution)/shard_map/all_to_all | solution.py:197
  79.8 1.5 copy-start
  171.8 16.2 %collective-permute-start.6 = (f32[6,2,144,1]{2,3,1,0:T(1,128)S(1)}, f32[6,2,144,1]{2,3,1,0:T(1,128)S(1)}, u32[]{:S(2)}, u32[]{:S(2)}) collective-permute-start(f32[6,2,144,1]{2,3,1,0:T(1,128)S(1)} %get-tuple-element.77), channel_id=1, source_target_pairs={{16,0},{32,16},{48,32},{64,48},{80,64},{96,80},{112,96},{128,112},... | collective-permute-start | bytes 20744 | tf_op jit(solution)/shard_map/ppermute | solution.py:22
  173.7 14.3 %collective-permute-start.7 = (f32[6,2,144,1]{2,3,1,0:T(1,128)S(1)}, f32[6,2,144,1]{2,3,1,0:T(1,128)S(1)}, u32[]{:S(2)}, u32[]{:S(2)}) collective-permute-start(f32[6,2,144,1]{2,3,1,0:T(1,128)S(1)} %get-tuple-element.78), channel_id=1, source_target_pairs={{0,16},{16,32},{32,48},{48,64},{64,80},{80,96},{96,112},{112,128},... | collective-permute-start | bytes 20744 | tf_op jit(solution)/shard_map/ppermute | solution.py:19
  179.4 1.6 collective-permute-start.4
  180.0 6.9 %collective-permute-start.5 = (f32[6,2,1,128]{3,1,2,0:T(2,128)S(1)}, f32[6,2,1,128]{3,1,2,0:T(2,128)S(1)}, u32[]{:S(2)}, u32[]{:S(2)}) collective-permute-start(f32[6,2,1,128]{3,1,2,0:T(2,128)S(1)} %copy.267), channel_id=1, source_target_pairs={{0,1},{1,2},{2,3},{3,4},{4,5},{5,6},{6,7},{7,8},{8,9},{9,10},{10,1... | collective-permute-start | bytes 18440 | tf_op jit(solution)/shard_map/ppermute | solution.py:19
  246.4 1.5 copy-start.1
  338.3 16.5 %collective-permute-start.10 = (f32[6,2,144,1]{2,3,1,0:T(1,128)S(1)}, f32[6,2,144,1]{2,3,1,0:T(1,128)S(1)}, u32[]{:S(2)}, u32[]{:S(2)}) collective-permute-start(f32[6,2,144,1]{2,3,1,0:T(1,128)S(1)} %get-tuple-element.73), channel_id=1, source_target_pairs={{16,0},{32,16},{48,32},{64,48},{80,64},{96,80},{112,96},{128,112},... | collective-permute-start | bytes 20744 | tf_op jit(solution)/shard_map/ppermute | solution.py:22
  340.2 14.6 %collective-permute-start.11 = (f32[6,2,144,1]{2,3,1,0:T(1,128)S(1)}, f32[6,2,144,1]{2,3,1,0:T(1,128)S(1)}, u32[]{:S(2)}, u32[]{:S(2)}) collective-permute-start(f32[6,2,144,1]{2,3,1,0:T(1,128)S(1)} %get-tuple-element.74), channel_id=1, source_target_pairs={{0,16},{16,32},{32,48},{48,64},{64,80},{80,96},{96,112},{112,128},... | collective-permute-start | bytes 20744 | tf_op jit(solution)/shard_map/ppermute | solution.py:19
  345.9 1.6 collective-permute-start.8
  346.5 7.1 %collective-permute-start.9 = (f32[6,2,1,128]{3,1,2,0:T(2,128)S(1)}, f32[6,2,1,128]{3,1,2,0:T(2,128)S(1)}, u32[]{:S(2)}, u32[]{:S(2)}) collective-permute-start(f32[6,2,1,128]{3,1,2,0:T(2,128)S(1)} %copy.276), channel_id=1, source_target_pairs={{0,1},{1,2},{2,3},{3,4},{4,5},{5,6},{6,7},{7,8},{8,9},{9,10},{10,1... | collective-permute-start | bytes 18440 | tf_op jit(solution)/shard_map/ppermute | solution.py:19
  413.1 1.5 copy-start.2
where the time goes:
time: 514 us; the launch traced here: 507 us
  local copies, waits for them, and re-layouts  226 us (44%)
  blocking collectives  98.4 us (19%)
  other arithmetic  65.3 us (13%)
  matrix products  54.4 us (11%)
  starting transfers between devices  33.4 us (6%)
  waiting for transfers between devices  26.6 us (5%)
    unnamed x22, local copies, waits for them, and re-layouts  96.9 us
    all_to_all x3, blocking collectives, filter_sector(): lax.all_to_all(damped, 'lon', split_axis=1, concat_axis=2, tiled=True)  57.8 us
    all_to_all x2, blocking collectives, local(): lax.all_to_all(flattened, 'lon', split_axis=2, concat_axis=1, tiled=True)  40.6 us
    mul x3, other arithmetic, local(): fields_now = fields_now + time_step * filtered.reshape(fields_now.shape)  25.4 us
    mul x3, local copies, waits for them, and re-layouts, local(): fields_now = fields_now + time_step * filtered.reshape(fields_now.shape)  24.3 us
    mul x9, local copies, waits for them, and re-layouts, smooth(): spec_re.reshape(vectors, slab_rows, total) * factors  22 us
    all_to_all x7, local copies, waits for them, and re-layouts, local(): lax.all_to_all(flattened, 'lon', split_axis=2, concat_axis=1, tiled=True)  18.3 us
    ppermute x6, starting transfers between devices, with_halo(): lax.ppermute(lax.slice_in_dim(block, block.shape[dim] - width, None, axis...  16.6 us
  transfers between devices with their start and end apart: 13, of which 5 were waited for; matrix products, arithmetic and copies ran while one was open for 2% of the time, Pallas kernels for 0%

commit v1 on v0

--- a/solution.py
+++ b/solution.py
@@ -191,7 +191,12 @@
             damped = lax.cond(
                 is_polar, lambda inner: smooth(inner, start_row), lambda inner: inner, sector
             )
-            return lax.all_to_all(damped, "lon", split_axis=1, concat_axis=2, tiled=True)
+            return jnp.concatenate(
+                lax.all_to_all(
+                    jnp.stack(jnp.split(damped, lax.axis_size("lon"), axis=1)), "lon", 0, 0
+                ),
+                axis=2,
+            )
 
         filtered = filter_sector(
             lax.all_to_all(flattened, "lon", split_axis=2, concat_axis=1, tiled=True)

time: 514 us -> 367 us (0.71)
  local copies, waits for them, and re-layouts: 226 us -> 104 us
  other arithmetic: 65.3 us -> 19 us
  blocking collectives: 98.4 us -> 120 us
    unnamed x22 -> x83, local copies, waits for them, and re-layouts: 96.9 us -> 20.9 us
    mul x3, other arithmetic: 25.4 us -> 0.46 us  [local(): fields_now = fields_now + time_step * filtered.reshape(fields_now.shape)]
    mul x3, local copies, waits for them, and re-layouts: 24.3 us -> 0.39 us  [local(): fields_now = fields_now + time_step * filtered.reshape(fields_now.shape)]
    all_to_all x3, blocking collectives: 57.8 us -> 78.7 us  [filter_sector(): lax.all_to_all(jnp.stack(jnp.split(damped, lax.axis_size('lon'), axis=1))...]
    cond x15 -> x12, local copies, waits for them, and re-layouts: 18.4 us -> 2.14 us  [the longest x3 16.2 us: filter_sector(): lax.cond(is_polar, lambda inner: smooth(inner, start_row), lambda inner:...]
    all_to_all x3 -> x0, other arithmetic: 11.6 us -> none  [filter_sector(): lax.all_to_all(damped, 'lon', split_axis=1, concat_axis=2, tiled=True)]
  transfers between devices with their start and end apart: 13 -> 13, of which waited for: 5 -> 6; matrix products, arithmetic and copies ran while one was open for 2% -> 1% of each run, Pallas kernels for 0% -> 0%
where the time goes in v1:
time: 367 us; the launch traced here: 360 us
  blocking collectives  120 us (33%)
  local copies, waits for them, and re-layouts  104 us (28%)
  matrix products  54.3 us (15%)
  starting transfers between devices  32.5 us (9%)
  waiting for transfers between devices  28.4 us (8%)
  other arithmetic  19 us (5%)
    all_to_all x3, blocking collectives, filter_sector(): lax.all_to_all(jnp.stack(jnp.split(damped, lax.axis_size('lon'), axis=1))...  78.7 us
    all_to_all x2, blocking collectives, local(): lax.all_to_all(flattened, 'lon', split_axis=2, concat_axis=1, tiled=True)  40.9 us
    unnamed x83, local copies, waits for them, and re-layouts  20.9 us
    mul x9, local copies, waits for them, and re-layouts, smooth(): spec_re.reshape(vectors, slab_rows, total) * factors  18.9 us
    all_to_all x7, local copies, waits for them, and re-layouts, local(): lax.all_to_all(flattened, 'lon', split_axis=2, concat_axis=1, tiled=True)  18.3 us
    ppermute x6, starting transfers between devices, with_halo(): lax.ppermute(lax.slice_in_dim(block, block.shape[dim] - width, None, axis...  16.5 us
    all_to_all x1, waiting for transfers between devices, local(): lax.all_to_all(flattened, 'lon', split_axis=2, concat_axis=1, tiled=True)  16.2 us
    reshape x6, local copies, waits for them, and re-layouts, forward_real(): grid = signal.reshape(vectors, outer, inner)  15.7 us
  transfers between devices with their start and end apart: 13, of which 6 were waited for; matrix products, arithmetic and copies ran while one was open for 1% of the time, Pallas kernels for 0%

profile of v1, /device:TPU:96, one launch (start us, length us, event | category | flops | bytes accessed | tf_op | source)
XLA Modules:
  0.0 359.9 jit_solution(7687619554726092583)
XLA Ops:
  1.0 5.3 %collective-permute-start = (f32[6,2,1,128]{3,1,2,0:T(2,128)S(1)}, f32[6,2,1,128]{3,1,2,0:T(2,128)S(1)}, u32[]{:S(2)}, u32[]{:S(2)}) collective-permute-start(f32[6,2,1,128]{3,1,2,0:T(2,128)S(1)} %bitcast.432), channel_id=1, source_target_pairs={{1,0},{2,1},{3,2},{4,3},{5,4},{6,5},{7,6},{8,7},{9,8},{10,9},{11,1... | collective-permute-start | bytes 18440 | tf_op jit(solution)/shard_map/ppermute | solution.py:22
  10.0 5.0 %collective-permute-start.3 = (f32[6,2,144,1]{2,3,1,0:T(1,128)S(1)}, f32[6,2,144,1]{2,3,1,0:T(1,128)S(1)}, u32[]{:S(2)}, u32[]{:S(2)}) collective-permute-start(f32[6,2,144,1]{2,3,1,0:T(1,128)S(1)} %get-tuple-element.470), channel_id=1, source_target_pairs={{0,16},{16,32},{32,48},{48,64},{64,80},{80,96},{96,112},{112,128},... | collective-permute-start | bytes 20744 | tf_op jit(solution)/shard_map/ppermute | solution.py:19
  21.6 3.9 %reshape.286 = f32[16,1,13824]{2,1,0:T(1,128)} reshape(f32[128,12,144]{2,1,0:T(8,128)} %bitcast.413) | data formatting | bytes 1769472
  25.4 4.7 %all-to-all-start = ((f32[16,1,13824]{2,1,0:T(1,128)}), f32[16,1,13824]{2,1,0:T(1,128)S(1)}, u32[]{:S(2)}, u32[]{:S(2)}) async-start(f32[16,1,13824]{2,1,0:T(1,128)} %reshape.286), calls=%async_computation | async-start | bytes 1769472 | tf_op jit(solution)/shard_map/all_to_all | solution.py:202
  30.2 16.2 %all-to-all-done = f32[16,1,13824]{2,1,0:T(1,128)S(1)} async-done(((f32[16,1,13824]{2,1,0:T(1,128)}), f32[16,1,13824]{2,1,0:T(1,128)S(1)}, u32[]{:S(2)}, u32[]{:S(2)}) %all-to-all-start) | async-done | bytes 884768 | tf_op jit(solution)/shard_map/all_to_all | solution.py:202
  52.1 3.7 %copy.189 = f32[12,16,144,8]{2,1,3,0:T(8,128)} copy(f32[12,16,144,8]{2,0,3,1:T(8,128)} %bitcast.414) | data formatting | bytes 1769472 | tf_op jit(solution)/shard_map/all_to_all | solution.py:202
  58.0 35.6 %conditional.3 = (f32[1,12,144,8]{2,3,1,0:T(8,128)S(1)}, f32[1,12,144,8]{2,3,1,0:T(8,128)S(1)}, f32[1,12,144,8]{2,3,1,0:T(8,128)S(1)}, f32[1,12,144,8]{2,3,1,0:T...) conditional(s32[]{:T(128)} %convert_element_type.252, ...), branch_computations={%region_0.0_spmd, %region_1.2_spmd} | conditional | flops 1533790208 | bytes 48321928 | solution.py:191
  93.9 26.2 %all_to_all.81 = f32[16,12,144,8]{2,3,1,0:T(8,128)S(1)} all-to-all(f32[16,12,144,8]{2,3,1,0:T(8,128)S(1)} %constant_dynamic-update-slice_fusion), channel_id=1, replica_groups=mesh['lat'=16,'lon'=16] {'lon'}, dimensions={0} | all-to-all | bytes 1769472 | tf_op jit(solution)/shard_map/all_to_all | solution.py:195
  122.6 5.1 %collective-permute-start.7 = (f32[6,2,144,1]{2,3,1,0:T(1,128)S(1)}, f32[6,2,144,1]{2,3,1,0:T(1,128)S(1)}, u32[]{:S(2)}, u32[]{:S(2)}) collective-permute-start(f32[6,2,144,1]{2,3,1,0:T(1,128)S(1)} %get-tuple-element.468), channel_id=1, source_target_pairs={{0,16},{16,32},{32,48},{48,64},{64,80},{80,96},{96,112},{112,128},... | collective-permute-start | bytes 20744 | tf_op jit(solution)/shard_map/ppermute | solution.py:19
  130.0 5.3 %collective-permute-done.5 = f32[6,2,1,128]{3,1,2,0:T(2,128)S(1)} collective-permute-done((f32[6,2,1,128]{3,1,2,0:T(2,128)S(1)}, f32[6,2,1,128]{3,1,2,0:T(2,128)S(1)}, u32[]{:S(2)}, u32[]{:S(2)}) %collective-permute-start.5) | collective-permute-done | bytes 6176 | tf_op jit(solution)/shard_map/ppermute | solution.py:19
  140.9 3.2 reshape.288
  144.0 20.4 %all_to_all.82 = f32[16,1,13824]{2,1,0:T(1,128)} all-to-all(f32[16,1,13824]{2,1,0:T(1,128)S(1)} %reshape.288), channel_id=1, replica_groups=mesh['lat'=16,'lon'=16] {'lon'}, dimensions={0} | all-to-all | bytes 1769472 | tf_op jit(solution)/shard_map/all_to_all | solution.py:202
  164.5 3.8 %reduce.1 = f32[16,13824]{1,0:T(8,128)S(1)} reduce(f32[16,1,13824]{2,1,0:T(1,128)} %all_to_all.82, f32[]{:T(128)} %broadcast.839), dimensions={1}, to_apply=%all_to_all.65.reduce_sub_computation | reduce | bytes 1769476 | tf_op jit(solution)/shard_map/all_to_all | solution.py:202
  170.8 3.7 %copy.198 = f32[12,16,144,8]{2,1,3,0:T(8,128)} copy(f32[12,16,144,8]{2,0,3,1:T(8,128)} %bitcast.416) | data formatting | bytes 1769472 | tf_op jit(solution)/shard_map/all_to_all | solution.py:202
  176.7 37.1 %conditional.4 = (f32[1,12,144,8]{2,3,1,0:T(8,128)S(1)}, f32[1,12,144,8]{2,3,1,0:T(8,128)S(1)}, f32[1,12,144,8]{2,3,1,0:T(8,128)S(1)}, f32[1,12,144,8]{2,3,1,0:T...) conditional(s32[]{:T(128)} %convert_element_type.252, ...), branch_computations={%region_2.3_spmd, %region_3.4_spmd} | conditional | flops 1533790208 | bytes 48321928 | solution.py:191
  178.9 3.5 mul.1141
  214.1 26.2 %all_to_all.83 = f32[16,12,144,8]{2,3,1,0:T(8,128)S(1)} all-to-all(f32[16,12,144,8]{2,3,1,0:T(8,128)S(1)} %constant_dynamic-update-slice_fusion.16), channel_id=1, replica_groups=mesh['lat'=16,'lon'=16] {'lon'}, dimensions={0} | all-to-all | bytes 1769472 | tf_op jit(solution)/shard_map/all_to_all | solution.py:195
  242.8 5.1 %collective-permute-start.11 = (f32[6,2,144,1]{2,3,1,0:T(1,128)S(1)}, f32[6,2,144,1]{2,3,1,0:T(1,128)S(1)}, u32[]{:S(2)}, u32[]{:S(2)}) collective-permute-start(f32[6,2,144,1]{2,3,1,0:T(1,128)S(1)} %get-tuple-element.464), channel_id=1, source_target_pairs={{0,16},{16,32},{32,48},{48,64},{64,80},{80,96},{96,112},{112,128},... | collective-permute-start | bytes 20744 | tf_op jit(solution)/shard_map/ppermute | solution.py:19
  250.2 5.3 %collective-permute-done.9 = f32[6,2,1,128]{3,1,2,0:T(2,128)S(1)} collective-permute-done((f32[6,2,1,128]{3,1,2,0:T(2,128)S(1)}, f32[6,2,1,128]{3,1,2,0:T(2,128)S(1)}, u32[]{:S(2)}, u32[]{:S(2)}) %collective-permute-start.9) | collective-permute-done | bytes 6176 | tf_op jit(solution)/shard_map/ppermute | solution.py:19
  261.0 3.2 reshape.290
  264.2 20.5 %all_to_all.84 = f32[16,1,13824]{2,1,0:T(1,128)S(1)} all-to-all(f32[16,1,13824]{2,1,0:T(1,128)S(1)} %reshape.290), channel_id=1, replica_groups=mesh['lat'=16,'lon'=16] {'lon'}, dimensions={0} | all-to-all | bytes 1769472 | tf_op jit(solution)/shard_map/all_to_all | solution.py:202
  289.9 3.7 %copy.206 = f32[12,16,144,8]{2,1,3,0:T(8,128)} copy(f32[12,16,144,8]{2,0,3,1:T(8,128)} %bitcast.418) | data formatting | bytes 1769472 | tf_op jit(solution)/shard_map/all_to_all | solution.py:202
  295.8 35.4 %conditional.5 = (f32[1,12,144,8]{2,3,1,0:T(8,128)S(1)}, f32[1,12,144,8]{2,3,1,0:T(8,128)S(1)}, f32[1,12,144,8]{2,3,1,0:T(8,128)S(1)}, f32[1,12,144,8]{2,3,1,0:T...) conditional(s32[]{:T(128)} %convert_element_type.252, ...), branch_computations={%region_4.5_spmd, %region_5.6_spmd} | conditional | flops 1533790208 | bytes 48321928 | solution.py:191
  331.5 26.2 %all_to_all.85 = f32[16,12,144,8]{2,3,1,0:T(8,128)S(1)} all-to-all(f32[16,12,144,8]{2,3,1,0:T(8,128)S(1)} %constant_dynamic-update-slice_fusion.32), channel_id=1, replica_groups=mesh['lat'=16,'lon'=16] {'lon'}, dimensions={0} | all-to-all | bytes 1769472 | tf_op jit(solution)/shard_map/all_to_all | solution.py:195
  (244 shorter events, 157.2 us)
Async XLA Ops:
  0.0 15.2 %copy-start.17 = (f32[2,128]{1,0:T(2,128)S(1)}, f32[2,128]{1,0:T(2,128)}, u32[]{:S(2)}) copy-start(f32[2,128]{1,0:T(2,128)} %param.13) | copy-start | bytes 3076
  0.0 15.2 %copy-start.16 = (f32[3,2]{0,1:T(2,128)S(1)}, f32[3,2]{0,1:T(2,128)}, u32[]{:S(2)}) copy-start(f32[3,2]{0,1:T(2,128)} %param.15) | copy-start | bytes 76
  0.9 14.8 %collective-permute-start.1 = (f32[6,2,1,128]{3,1,2,0:T(2,128)S(1)}, f32[6,2,1,128]{3,1,2,0:T(2,128)S(1)}, u32[]{:S(2)}, u32[]{:S(2)}) collective-permute-start(f32[6,2,1,128]{3,1,2,0:T(2,128)S(1)} %bitcast.431), channel_id=1, source_target_pairs={{0,1},{1,2},{2,3},{3,4},{4,5},{5,6},{6,7},{7,8},{8,9},{9,10},{10,1... | collective-permute-start | bytes 18440 | tf_op jit(solution)/shard_map/ppermute | solution.py:19
  1.0 15.5 %copy-start.3 = (f32[2,128]{1,0:T(2,128)S(1)}, f32[2,128]{1,0:T(2,128)}, u32[]{:S(2)}) copy-start(f32[2,128]{1,0:T(2,128)} %param.12) | copy-start | bytes 3076
  1.0 14.4 %collective-permute-start = (f32[6,2,1,128]{3,1,2,0:T(2,128)S(1)}, f32[6,2,1,128]{3,1,2,0:T(2,128)S(1)}, u32[]{:S(2)}, u32[]{:S(2)}) collective-permute-start(f32[6,2,1,128]{3,1,2,0:T(2,128)S(1)} %bitcast.432), channel_id=1, source_target_pairs={{1,0},{2,1},{3,2},{4,3},{5,4},{6,5},{7,6},{8,7},{9,8},{10,9},{11,1... | collective-permute-start | bytes 18440 | tf_op jit(solution)/shard_map/ppermute | solution.py:22
  8.0 8.0 %collective-permute-start.2 = (f32[6,2,144,1]{2,3,1,0:T(1,128)S(1)}, f32[6,2,144,1]{2,3,1,0:T(1,128)S(1)}, u32[]{:S(2)}, u32[]{:S(2)}) collective-permute-start(f32[6,2,144,1]{2,3,1,0:T(1,128)S(1)} %get-tuple-element.469), channel_id=1, source_target_pairs={{16,0},{32,16},{48,32},{64,48},{80,64},{96,80},{112,96},{128,112},... | collective-permute-start | bytes 20744 | tf_op jit(solution)/shard_map/ppermute | solution.py:22
  10.0 6.4 %collective-permute-start.3 = (f32[6,2,144,1]{2,3,1,0:T(1,128)S(1)}, f32[6,2,144,1]{2,3,1,0:T(1,128)S(1)}, u32[]{:S(2)}, u32[]{:S(2)}) collective-permute-start(f32[6,2,144,1]{2,3,1,0:T(1,128)S(1)} %get-tuple-element.470), channel_id=1, source_target_pairs={{0,16},{16,32},{32,48},{48,64},{64,80},{80,96},{96,112},{112,128},... | collective-permute-start | bytes 20744 | tf_op jit(solution)/shard_map/ppermute | solution.py:19
  15.2 3.3 copy-start.7
  15.2 3.3 copy-start.10
  15.3 3.2 copy-start.13
  25.4 21.0 %all-to-all-start = ((f32[16,1,13824]{2,1,0:T(1,128)}), f32[16,1,13824]{2,1,0:T(1,128)S(1)}, u32[]{:S(2)}, u32[]{:S(2)}) async-start(f32[16,1,13824]{2,1,0:T(1,128)} %reshape.286), calls=%async_computation | async-start | bytes 1769472 | tf_op jit(solution)/shard_map/all_to_all | solution.py:202
  73.3 1.5 copy-start
  120.7 15.0 %collective-permute-start.6 = (f32[6,2,144,1]{2,3,1,0:T(1,128)S(1)}, f32[6,2,144,1]{2,3,1,0:T(1,128)S(1)}, u32[]{:S(2)}, u32[]{:S(2)}) collective-permute-start(f32[6,2,144,1]{2,3,1,0:T(1,128)S(1)} %get-tuple-element.467), channel_id=1, source_target_pairs={{16,0},{32,16},{48,32},{64,48},{80,64},{96,80},{112,96},{128,112},... | collective-permute-start | bytes 20744 | tf_op jit(solution)/shard_map/ppermute | solution.py:22
  122.6 13.0 %collective-permute-start.7 = (f32[6,2,144,1]{2,3,1,0:T(1,128)S(1)}, f32[6,2,144,1]{2,3,1,0:T(1,128)S(1)}, u32[]{:S(2)}, u32[]{:S(2)}) collective-permute-start(f32[6,2,144,1]{2,3,1,0:T(1,128)S(1)} %get-tuple-element.468), channel_id=1, source_target_pairs={{0,16},{16,32},{32,48},{48,64},{64,80},{80,96},{96,112},{112,128},... | collective-permute-start | bytes 20744 | tf_op jit(solution)/shard_map/ppermute | solution.py:19
  128.3 1.4 collective-permute-start.4
  128.6 6.7 %collective-permute-start.5 = (f32[6,2,1,128]{3,1,2,0:T(2,128)S(1)}, f32[6,2,1,128]{3,1,2,0:T(2,128)S(1)}, u32[]{:S(2)}, u32[]{:S(2)}) collective-permute-start(f32[6,2,1,128]{3,1,2,0:T(2,128)S(1)} %copy.194), channel_id=1, source_target_pairs={{0,1},{1,2},{2,3},{3,4},{4,5},{5,6},{6,7},{7,8},{8,9},{9,10},{10,1... | collective-permute-start | bytes 18440 | tf_op jit(solution)/shard_map/ppermute | solution.py:19
  137.5 0.7 copy-start.14
  193.6 1.5 copy-start.1
  240.9 15.0 %collective-permute-start.10 = (f32[6,2,144,1]{2,3,1,0:T(1,128)S(1)}, f32[6,2,144,1]{2,3,1,0:T(1,128)S(1)}, u32[]{:S(2)}, u32[]{:S(2)}) collective-permute-start(f32[6,2,144,1]{2,3,1,0:T(1,128)S(1)} %get-tuple-element.463), channel_id=1, source_target_pairs={{16,0},{32,16},{48,32},{64,48},{80,64},{96,80},{112,96},{128,112},... | collective-permute-start | bytes 20744 | tf_op jit(solution)/shard_map/ppermute | solution.py:22
  242.8 13.0 %collective-permute-start.11 = (f32[6,2,144,1]{2,3,1,0:T(1,128)S(1)}, f32[6,2,144,1]{2,3,1,0:T(1,128)S(1)}, u32[]{:S(2)}, u32[]{:S(2)}) collective-permute-start(f32[6,2,144,1]{2,3,1,0:T(1,128)S(1)} %get-tuple-element.464), channel_id=1, source_target_pairs={{0,16},{16,32},{32,48},{48,64},{64,80},{80,96},{96,112},{112,128},... | collective-permute-start | bytes 20744 | tf_op jit(solution)/shard_map/ppermute | solution.py:19
  248.5 1.4 collective-permute-start.8
  248.8 6.7 %collective-permute-start.9 = (f32[6,2,1,128]{3,1,2,0:T(2,128)S(1)}, f32[6,2,1,128]{3,1,2,0:T(2,128)S(1)}, u32[]{:S(2)}, u32[]{:S(2)}) collective-permute-start(f32[6,2,1,128]{3,1,2,0:T(2,128)S(1)} %copy.202), channel_id=1, source_target_pairs={{0,1},{1,2},{2,3},{3,4},{4,5},{5,6},{6,7},{7,8},{8,9},{9,10},{10,1... | collective-permute-start | bytes 18440 | tf_op jit(solution)/shard_map/ppermute | solution.py:19
  257.6 0.7 copy-start.15
  311.0 1.5 copy-start.2
  (7 other events, 4.6 us)
